TPU v7x, 512 devices: a whole 4x8x8 slice. The times are simulated.
512 devices in a mesh: area: 128 (over z, y, core), blk: 4 (over x).
Axes of the slice: x: 4, y: 8, z: 8, core: 2. Of those that a mesh axis runs over, the one named last changes fastest.
Arguments:
- activity: float32 [1024, 4, 64, 128], P('area', 'blk'), may hold values from -8 to 8
- ext_input: bfloat16 [1024, 4, 64, 128], P('area', 'blk'), may hold values from -5 to 5
- weights: bfloat16 [384, 4, 128, 512], P('area', 'blk'), may hold values from -0.25 to 0.25
- slot_dst: int32 [384], P('area'), may hold values from 0 to 7
- slot_src: int32 [384], P('area'), may hold values from 0 to 1023, as said below
- slot_count: int32 [128], P('area'), may hold values from 3 to 3, as said below
- hebb_mask: int32 [384], P('area'), may hold values 0 or 1
Outputs:
- final_activity: float32 [1024, 4, 64, 128], P('area', 'blk')
- plasticity: bfloat16 [384, 4, 128, 512], P('area', 'blk')
Inputs may be any that keep to these rules, and one draw needn't show every extreme that they name: Index i of area holds area i // 4; sources lie in areas listed for it by a connectome over the areas that always lists the area itself, the areas beside it on both sides (counted round) and the opposite one. Slots 0, 1 and 2 of index i of area have their source sub-blocks held by indices (i - 1) mod 128, (i + 1) mod 128 and (i + 64) mod 128. Among the occupied slots of one index of area, at most 1 have source sub-blocks held by one index of area (slot_src // 8); some index of area reaches 1. `slot_count`: some index of area has all 3 slots occupied.
All inputs are finite; a program needn't handle non-finite values. No bound on the sum of `hebb_mask` on one device may be relied on, other than what follows from the above.
Results may differ from a plain program's by a relative error of at most 0.014.
Values may be sent and summed in bfloat16 or wider, within the bound.
No kernel may reach another device: no remote copies, remote signals or barrier semaphores. Data moves between devices by JAX's collectives and lax.ppermute only.
A program may use at most 64 MiB of HBM per device.

v0:
```python
import jax
import jax.numpy as jnp
from jax import lax
from jax.sharding import PartitionSpec as P

STEPS = 4
euler_step = 0.5


def request_rosters(src_rows, count_now, sub_dev, n_areas, link_cap):
    slot_cap = src_rows.shape[0]
    slot_ids = jnp.arange(slot_cap)
    occupied = slot_ids < count_now
    owner_idx = src_rows // sub_dev
    local_idx = src_rows % sub_dev
    earlier = (
        (owner_idx[:, None] == owner_idx[None, :])
        & occupied[None, :]
        & (slot_ids[None, :] < slot_ids[:, None])
    )
    link_idx = jnp.minimum(jnp.sum(earlier.astype(jnp.int32), axis=1), link_cap - 1)
    matches = (
        occupied[:, None, None]
        & (owner_idx[:, None, None] == jnp.arange(n_areas)[None, :, None])
        & (link_idx[:, None, None] == jnp.arange(link_cap)[None, None, :])
    )
    request_table = jnp.sum(jnp.where(matches, (local_idx + 1)[:, None, None], 0), axis=0)
    return (occupied, owner_idx, link_idx, request_table)


def body(activity, ext_input, weights, slot_dst, slot_src, slot_count, hebb_mask):
    n_areas = lax.axis_size("area")
    my_blk = lax.axis_index("blk")
    sub_dev = activity.shape[0]
    trials = activity.shape[2]
    quarter = activity.shape[3]
    slot_cap = slot_src.shape[0]
    sub_width = weights.shape[3]
    link_cap = (slot_cap + n_areas - 1) // n_areas
    occupied, owner_idx, link_idx, request_table = request_rosters(
        slot_src, slot_count[0], sub_dev, n_areas, link_cap
    )
    needed_rows = lax.all_to_all(request_table, "area", split_axis=0, concat_axis=0, tiled=True)
    is_valid = needed_rows > 0
    pick_idx = jnp.maximum(needed_rows - 1, 0)
    select = ((slot_dst[:, None] == jnp.arange(sub_dev)[None, :]) & occupied[:, None]).astype(
        jnp.float32
    )
    slot_weights = weights[:, 0]
    pre_list = []
    post_list = []
    full_act, full_ext = (
        lax.all_gather(activity.astype(jnp.bfloat16), "blk", axis=1, tiled=True).astype(
            activity.dtype
        ),
        lax.all_gather(
            ext_input.astype(jnp.float32).astype(jnp.bfloat16), "blk", axis=1, tiled=True
        ).astype(jnp.float32),
    )
    current = full_act.transpose(0, 2, 1, 3).reshape(sub_dev, trials, sub_width)
    drive_in = full_ext.transpose(0, 2, 1, 3).reshape(sub_dev, trials, sub_width)
    rate_full = jnp.tanh(current).astype(jnp.bfloat16)
    for step_idx in range(STEPS):
        rates_own = lax.dynamic_slice_in_dim(rate_full, my_blk * quarter, quarter, 2)
        outbound_rates = jnp.where(
            is_valid[:, :, None, None], rates_own[pick_idx], jnp.zeros((), jnp.bfloat16)
        )
        presynaptic_rates = lax.all_to_all(
            outbound_rates, "area", split_axis=0, concat_axis=0, tiled=True
        )[owner_idx, link_idx]
        input_contribution = jnp.einsum(
            "xvy,xye->xve", presynaptic_rates, slot_weights, preferred_element_type=jnp.float32
        )
        partial_value = jnp.einsum(
            "kd,kts->dts", select, input_contribution, precision=lax.Precision.HIGHEST
        )
        partial_value, presynaptic_rates = (partial_value, presynaptic_rates)
        summed = lax.psum(partial_value.astype(jnp.bfloat16), "blk").astype(jnp.float32)
        current = current + euler_step * (summed - current + drive_in)
        rate_full = jnp.tanh(current).astype(jnp.bfloat16)
        pre_list.append(presynaptic_rates)
        post_list.append(rate_full)
    final_state = lax.dynamic_slice_in_dim(current, my_blk * quarter, quarter, 2)[:, None]
    pre_all = jnp.stack(pre_list, axis=1).astype(jnp.float32)
    pre_centered = (pre_all - jnp.mean(pre_all, axis=2, keepdims=True)).astype(jnp.bfloat16)
    pre_centered = pre_centered.reshape(slot_cap, STEPS * trials, quarter)
    post_all = jnp.stack(post_list, axis=1).astype(jnp.float32)
    post_centered = (post_all - jnp.mean(post_all, axis=2, keepdims=True)).astype(jnp.bfloat16)
    post_slot = post_centered[slot_dst].reshape(slot_cap, STEPS * trials, sub_width)
    change = jnp.einsum("knq,kns->kqs", pre_centered, post_slot, preferred_element_type=jnp.float32)
    gate_on = (occupied & (hebb_mask == 1)).astype(jnp.float32)
    norm_scale = (STEPS * trials) ** (-0.5)
    plasticity = (change * gate_on[:, None, None] * norm_scale).astype(jnp.bfloat16)[:, None]
    return (final_state, plasticity)


def solution(mesh):
    in_specs = (
        P("area", "blk", None, None),
        P("area", "blk", None, None),
        P("area", "blk", None, None),
        P("area"),
        P("area"),
        P("area"),
        P("area"),
    )
    out_specs = (P("area", "blk", None, None), P("area", "blk", None, None))
    return jax.shard_map(body, mesh=mesh, in_specs=in_specs, out_specs=out_specs, check_vma=False)
```

profile of v0, /device:TPU:8, one launch (start us, length us, event | category | flops | bytes accessed | tf_op | source)
XLA Modules:
  0.0 565.2 jit_solution(8893313728588876898)
XLA Ops:
  7.9 0.7 fusion.35
  8.5 1.2 and_convert_fusion
  9.7 0.2 convert_reduce_fusion.2
  9.9 0.6 copy-done.13
  10.5 0.1 fusion.34
  10.6 0.7 copy.91
  11.3 17.4 %all-to-all-start = ((s32[128,1,1]{2,1,0:T(1,128)}), s32[128,1,1]{2,1,0:T(1,128)S(1)}, u32[]{:S(2)}, u32[]{:S(2)}) async-start(s32[128,1,1]{2,1,0:T(1,128)} %copy.91), calls=%async_computation | async-start | bytes 131072 | tf_op jit(solution)/shard_map/all_to_all | solution.py:43
  28.7 1.0 convert_element_type.74
  29.7 13.1 %all_gather.6 = bf16[8,4,64,128]{3,2,1,0:T(8,128)(2,1)S(1)} all-gather(bf16[8,1,64,128]{3,2,1,0:T(8,128)(2,1)S(1)} %convert_element_type.74), channel_id=1, replica_groups=mesh['area'=128,'blk'=4] {'blk'}, dimensions={1}, use_global_device_ids=true | all-gather | bytes 655360 | tf_op jit(solution)/shard_map/all_gather | solution.py:53
  42.8 0.1 convert_bitcast_fusion.1
  43.0 0.6 copy.153
  43.6 0.1 fusion.30
  43.7 2.4 maximum_reduce_fusion
  46.0 2.2 gather_fusion
  48.2 2.4 compare_reduce_fusion
  50.6 3.2 fusion.4
  53.7 13.7 %all-to-all-start.1 = ((bf16[128,1,64,128]{3,2,1,0:T(8,128)(2,1)}), bf16[128,1,64,128]{3,2,1,0:T(8,128)(2,1)S(1)}, u32[]{:S(2)}, u32[]{:S(2)}) async-start(bf16[128,1,64,128]{3,2,1,0:T(8,128)(2,1)} %fusion.4), calls=%async_computation.1 | async-start | bytes 4194304 | tf_op jit(solution)/shard_map/all_to_all | solution.py:68
  67.5 0.7 fusion.42
  68.2 0.7 fusion.32
  68.9 52.5 %all-to-all-done.1 = bf16[128,1,64,128]{3,2,1,0:T(8,128)(2,1)S(1)} async-done(((bf16[128,1,64,128]{3,2,1,0:T(8,128)(2,1)}), bf16[128,1,64,128]{3,2,1,0:T(8,128)(2,1)S(1)}, u32[]{:S(2)}, u32[]{:S(2)}) %all-to-all-start.1) | async-done | bytes 2097184 | tf_op jit(solution)/shard_map/all_to_all | solution.py:68
  121.5 1.2 gather_fusion.1
  122.7 1.0 fusion.28
  123.7 1.7 convolution_convert_fusion.3
  125.5 14.4 %all_gather.7 = bf16[8,4,64,128]{3,2,1,0:T(8,128)(2,1)S(1)} all-gather(bf16[8,1,64,128]{3,2,1,0:T(8,128)(2,1)S(1)} %copy-done.10), channel_id=1, replica_groups=mesh['area'=128,'blk'=4] {'blk'}, dimensions={1}, use_global_device_ids=true | all-gather | bytes 655360 | tf_op jit(solution)/shard_map/all_gather | solution.py:56
  139.8 0.1 convert_bitcast_fusion
  140.0 32.7 %all-reduce.5.cloned.1.call-done = bf16[8,64,512]{2,0,1:T(8,128)(2,1)} async-done(((bf16[8,64,512]{2,0,1:T(8,128)(2,1)}), bf16[8,64,512]{2,0,1:T(8,128)(2,1)}) %all-reduce.5.cloned.1.call-update) | async-done | bytes 524304 | tf_op jit(solution)/shard_map/psum | solution.py:78
  172.6 2.2 tanh_convert_fusion.3
  174.9 0.8 copy-done.4
  175.7 2.2 gather_fusion.2
  177.9 1.8 fusion.3
  179.7 68.1 %all_to_all.29 = bf16[128,1,64,128]{3,2,1,0:T(8,128)(2,1)} all-to-all(bf16[128,1,64,128]{3,2,1,0:T(8,128)(2,1)S(1)} %fusion.3), channel_id=1, replica_groups=mesh['area'=128,'blk'=4] {'area'}, dimensions={0} | all-to-all | bytes 4194304 | tf_op jit(solution)/shard_map/all_to_all | solution.py:68
  247.8 2.2 gather_fusion.3
  250.0 0.2 fusion.26
  250.2 1.7 convolution_convert_fusion.2
  252.0 46.3 %all-reduce.7.cloned.1.call-done = bf16[8,64,512]{2,0,1:T(8,128)(2,1)} async-done(((bf16[8,64,512]{2,0,1:T(8,128)(2,1)}), bf16[8,64,512]{2,0,1:T(8,128)(2,1)}) %all-reduce.7.cloned.1.call-update) | async-done | bytes 524304 | tf_op jit(solution)/shard_map/psum | solution.py:78
  298.3 2.3 tanh_convert_fusion.2
  300.6 0.8 copy-done.2
  301.4 2.2 gather_fusion.4
  303.6 1.8 fusion.2
  305.4 68.1 %all_to_all.30 = bf16[128,1,64,128]{3,2,1,0:T(8,128)(2,1)} all-to-all(bf16[128,1,64,128]{3,2,1,0:T(8,128)(2,1)S(1)} %fusion.2), channel_id=1, replica_groups=mesh['area'=128,'blk'=4] {'area'}, dimensions={0} | all-to-all | bytes 4194304 | tf_op jit(solution)/shard_map/all_to_all | solution.py:68
  373.5 2.2 gather_fusion.5
  375.6 0.2 fusion.24
  375.8 1.7 convolution_convert_fusion.1
  377.5 46.4 %all-reduce.9.cloned.1.call-done = bf16[8,64,512]{2,0,1:T(8,128)(2,1)} async-done(((bf16[8,64,512]{2,0,1:T(8,128)(2,1)}), bf16[8,64,512]{2,0,1:T(8,128)(2,1)}) %all-reduce.9.cloned.1.call-update) | async-done | bytes 524304 | tf_op jit(solution)/shard_map/psum | solution.py:78
  423.9 2.6 tanh_convert_fusion.1
  426.5 0.8 copy-done.6
  427.3 2.1 gather_fusion.6
  429.5 3.1 fusion.1
  432.6 15.0 %all-to-all-start.4 = ((bf16[128,1,64,128]{3,2,1,0:T(8,128)(2,1)}), bf16[128,1,64,128]{3,2,1,0:T(8,128)(2,1)}, u32[]{:S(2)}, u32[]{:S(2)}) async-start(bf16[128,1,64,128]{3,2,1,0:T(8,128)(2,1)} %fusion.1), calls=%async_computation.4 | async-start | bytes 4194304 | tf_op jit(solution)/shard_map/all_to_all | solution.py:68
  447.7 53.6 %all-to-all-done.4 = bf16[128,1,64,128]{3,2,1,0:T(8,128)(2,1)} async-done(((bf16[128,1,64,128]{3,2,1,0:T(8,128)(2,1)}), bf16[128,1,64,128]{3,2,1,0:T(8,128)(2,1)}, u32[]{:S(2)}, u32[]{:S(2)}) %all-to-all-start.4) | async-done | bytes 2097184 | tf_op jit(solution)/shard_map/all_to_all | solution.py:68
  501.2 2.2 gather_fusion.7
  503.4 0.2 fusion.22
  503.6 1.7 convolution_convert_fusion
  505.3 0.1 convert_reduce_fusion.1
  505.4 0.1 fusion.21
  505.4 0.7 copy.106
  506.1 45.5 %all-reduce.11.cloned.1.call-done = bf16[8,64,512]{2,0,1:T(8,128)(2,1)} async-done(((bf16[8,64,512]{2,0,1:T(8,128)(2,1)}), bf16[8,64,512]{2,0,1:T(8,128)(2,1)}) %all-reduce.11.cloned.1.call-update) | async-done | bytes 524304 | tf_op jit(solution)/shard_map/psum | solution.py:78
  551.7 3.0 fusion.16
  554.6 0.3 convert_reduce_fusion
  554.9 0.5 fusion
  555.5 0.7 copy.107
  556.2 0.8 copy.109
  557.0 0.6 gather_fusion.8
  557.6 1.1 fusion.7
  (49 shorter events, 0.5 us)
Async XLA Ops:
  7.2 115.5 %copy-start = (bf16[3,1,128,512]{3,2,1,0:T(8,128)(2,1)S(1)}, bf16[3,1,128,512]{3,2,1,0:T(8,128)(2,1)}, u32[]{:S(2)}) copy-start(bf16[3,1,128,512]{3,2,1,0:T(8,128)(2,1)} %param.9) | copy-start | bytes 1179652
  9.7 19.0 %copy-start.11 = (pred[3]{0:T(512)(128)(4,1)}, pred[3]{0:T(512)(128)(4,1)S(1)}, u32[]{:S(2)}) copy-start(pred[3]{0:T(512)(128)(4,1)S(1)} %get-tuple-element.19) | copy-start | bytes 13
  9.9 0.6 copy-start.13
  11.3 32.3 %all-to-all-start = ((s32[128,1,1]{2,1,0:T(1,128)}), s32[128,1,1]{2,1,0:T(1,128)S(1)}, u32[]{:S(2)}, u32[]{:S(2)}) async-start(s32[128,1,1]{2,1,0:T(1,128)} %copy.91), calls=%async_computation | async-start | bytes 131072 | tf_op jit(solution)/shard_map/all_to_all | solution.py:43
  53.7 67.8 %all-to-all-start.1 = ((bf16[128,1,64,128]{3,2,1,0:T(8,128)(2,1)}), bf16[128,1,64,128]{3,2,1,0:T(8,128)(2,1)S(1)}, u32[]{:S(2)}, u32[]{:S(2)}) async-start(bf16[128,1,64,128]{3,2,1,0:T(8,128)(2,1)} %fusion.4), calls=%async_computation.1 | async-start | bytes 4194304 | tf_op jit(solution)/shard_map/all_to_all | solution.py:68
  67.5 105.2 %all-reduce.5.cloned.1.call-start = ((), (), s32[]{:S(2)}) async-start(), calls=%async_computation.5 | async-start | bytes 1048576 | tf_op jit(solution)/shard_map/psum | solution.py:78
  122.7 2.8 copy-start.10
  125.4 172.9 %all-reduce.7.cloned.1.call-start = ((), (), s32[]{:S(2)}) async-start(), calls=%async_computation.6 | async-start | bytes 1048576 | tf_op jit(solution)/shard_map/psum | solution.py:78
  174.9 0.8 copy-start.4
  247.8 50.5 %copy-start.1 = (bf16[8,64,512]{2,0,1:T(8,128)(2,1)S(1)}, bf16[8,64,512]{2,0,1:T(8,128)(2,1)}, u32[]{:S(2)}) copy-start(bf16[8,64,512]{2,0,1:T(8,128)(2,1)} %all-reduce.5.cloned.1.call-done) | copy-start | bytes 1572868
  251.9 172.0 %all-reduce.9.cloned.1.call-start = ((), (), s32[]{:S(2)}) async-start(), calls=%async_computation.7 | async-start | bytes 1048576 | tf_op jit(solution)/shard_map/psum | solution.py:78
  300.6 0.8 copy-start.2
  426.5 0.8 copy-start.6
  432.6 15.0 %copy-start.14 = (s32[3]{0:T(128)S(1)}, s32[3]{0:T(128)}, u32[]{:S(2)}) copy-start(s32[3]{0:T(128)} %param.10) | copy-start | bytes 40
  432.6 68.6 %all-to-all-start.4 = ((bf16[128,1,64,128]{3,2,1,0:T(8,128)(2,1)}), bf16[128,1,64,128]{3,2,1,0:T(8,128)(2,1)}, u32[]{:S(2)}, u32[]{:S(2)}) async-start(bf16[128,1,64,128]{3,2,1,0:T(8,128)(2,1)} %fusion.1), calls=%async_computation.4 | async-start | bytes 4194304 | tf_op jit(solution)/shard_map/all_to_all | solution.py:68
  447.6 57.7 %copy-start.9 = (bf16[3,64,128]{2,1,0:T(8,128)(2,1)S(1)}, bf16[3,64,128]{2,1,0:T(8,128)(2,1)}, u32[]{:S(2)}) copy-start(bf16[3,64,128]{2,1,0:T(8,128)(2,1)} %gather_fusion.1) | copy-start | bytes 147460
  447.6 104.1 %all-reduce.11.cloned.1.call-start = ((), (), s32[]{:S(2)}) async-start(), calls=%async_computation.8 | async-start | bytes 1048576 | tf_op jit(solution)/shard_map/psum | solution.py:78
  551.7 3.0 copy-start.3
  551.7 3.0 copy-start.5
  551.7 3.0 copy-start.7
  556.2 1.4 copy-start.8
  556.2 1.4 copy-start.12
Sparse Core Ops, SparseCore 0:
  125.5 47.0 all-reduce.4
  252.0 46.2 all-reduce.6
  377.7 46.2 all-reduce.8
  505.4 46.2 all-reduce.10
where the time goes:
time: 566 us; the launch traced here: 565 us
  waiting for transfers between devices  277 us (49%)
  blocking collectives  164 us (29%)
  starting transfers between devices  46.2 us (8%)
  other arithmetic  30.4 us (5%)
  local copies, waits for them, and re-layouts  23.6 us (4%)
  between operations  14.9 us (3%)
  matrix products  9.37 us (2%)
    psum x4, waiting for transfers between devices, body(): lax.psum(partial_value.astype(jnp.bfloat16), 'blk').astype(jnp.float32)  171 us
    all_to_all x2, blocking collectives, body(): lax.all_to_all(outbound_rates, 'area', split_axis=0, concat_axis=0, tiled...  136 us
    all_to_all x2, waiting for transfers between devices, body(): lax.all_to_all(outbound_rates, 'area', split_axis=0, concat_axis=0, tiled...  106 us
    all_to_all x2, starting transfers between devices, body(): lax.all_to_all(outbound_rates, 'area', split_axis=0, concat_axis=0, tiled...  28.7 us
    all_to_all x1, starting transfers between devices, body(): lax.all_to_all(request_table, 'area', split_axis=0, concat_axis=0, tiled=...  17.4 us
    all_gather x1, blocking collectives, body(): lax.all_gather(ext_input.astype(jnp.float32).astype(jnp.bfloat16), 'blk',...  14.4 us
    all_gather x1, blocking collectives, body(): lax.all_gather(activity.astype(jnp.bfloat16), 'blk', axis=1, tiled=True)  13.1 us
  transfers between devices with their start and end apart: 7, of which 6 were waited for; matrix products, arithmetic and copies ran while one was open for 1% of the time, Pallas kernels for 0%

commit v1 on v0

--- a/solution.py
+++ b/solution.py
@@ -49,13 +49,22 @@
     slot_weights = weights[:, 0]
     pre_list = []
     post_list = []
+    patches_begin = lambda tile_in, a_name: jnp.concatenate(
+        jax.lax.all_to_all(
+            jnp.stack([tile_in] * jax.lax.psum(1, a_name), axis=0),
+            a_name,
+            split_axis=0,
+            concat_axis=0,
+        ),
+        1,
+    )
     full_act, full_ext = (
         lax.all_gather(activity.astype(jnp.bfloat16), "blk", axis=1, tiled=True).astype(
             activity.dtype
         ),
-        lax.all_gather(
-            ext_input.astype(jnp.float32).astype(jnp.bfloat16), "blk", axis=1, tiled=True
-        ).astype(jnp.float32),
+        patches_begin(ext_input.astype(jnp.float32).astype(jnp.bfloat16), "blk").astype(
+            jnp.float32
+        ),
     )
     current = full_act.transpose(0, 2, 1, 3).reshape(sub_dev, trials, sub_width)
     drive_in = full_ext.transpose(0, 2, 1, 3).reshape(sub_dev, trials, sub_width)

time: 566 us -> 563 us (level)
    all_to_all x0 -> x1, blocking collectives: none -> 15.5 us  [body(): jax.lax.all_to_all(jnp.stack([tile_in] * jax.lax.psum(1, a_name), axis=0)...]
    all_gather x1 -> x0, blocking collectives: 14.4 us -> none  [body(): lax.all_gather(ext_input.astype(jnp.float32).astype(jnp.bfloat16), 'blk',...]
where the time goes in v1:
time: 563 us; the launch traced here: 562 us
  waiting for transfers between devices  276 us (49%)
  blocking collectives  165 us (29%)
  starting transfers between devices  46.2 us (8%)
  other arithmetic  28.2 us (5%)
  local copies, waits for them, and re-layouts  22.9 us (4%)
  between operations  14.9 us (3%)
  matrix products  9.36 us (2%)
    psum x4, waiting for transfers between devices, body(): lax.psum(partial_value.astype(jnp.bfloat16), 'blk').astype(jnp.float32)  170 us
    all_to_all x2, blocking collectives, body(): lax.all_to_all(outbound_rates, 'area', split_axis=0, concat_axis=0, tiled...  136 us
    all_to_all x2, waiting for transfers between devices, body(): lax.all_to_all(outbound_rates, 'area', split_axis=0, concat_axis=0, tiled...  106 us
    all_to_all x2, starting transfers between devices, body(): lax.all_to_all(outbound_rates, 'area', split_axis=0, concat_axis=0, tiled...  28.5 us
    all_to_all x1, starting transfers between devices, body(): lax.all_to_all(request_table, 'area', split_axis=0, concat_axis=0, tiled=...  17.4 us
    all_to_all x1, blocking collectives, body(): jax.lax.all_to_all(jnp.stack([tile_in] * jax.lax.psum(1, a_name), axis=0)...  15.5 us
    all_gather x1, blocking collectives, body(): lax.all_gather(activity.astype(jnp.bfloat16), 'blk', axis=1, tiled=True)  13.1 us
  transfers between devices with their start and end apart: 7, of which 6 were waited for; matrix products, arithmetic and copies ran while one was open for 1% of the time, Pallas kernels for 0%

profile of v1, /device:TPU:8, one launch (start us, length us, event | category | flops | bytes accessed | tf_op | source)
XLA Modules:
  0.0 562.4 jit_solution(10849964323612475022)
XLA Ops:
  7.9 0.7 fusion.35
  8.5 1.2 and_convert_fusion
  9.8 0.2 convert_reduce_fusion.2
  10.0 0.5 copy-done.11
  10.5 0.1 fusion.34
  10.6 0.7 copy.93
  11.3 17.4 %all-to-all-start = ((s32[128,1,1]{2,1,0:T(1,128)}), s32[128,1,1]{2,1,0:T(1,128)S(1)}, u32[]{:S(2)}, u32[]{:S(2)}) async-start(s32[128,1,1]{2,1,0:T(1,128)} %copy.93), calls=%async_computation | async-start | bytes 131072 | tf_op jit(solution)/shard_map/all_to_all | solution.py:43
  28.7 1.0 convert_element_type.80
  29.7 13.1 %all_gather.3 = bf16[8,4,64,128]{3,2,1,0:T(8,128)(2,1)S(1)} all-gather(bf16[8,1,64,128]{3,2,1,0:T(8,128)(2,1)S(1)} %convert_element_type.80), channel_id=1, replica_groups=mesh['area'=128,'blk'=4] {'blk'}, dimensions={1}, use_global_device_ids=true | all-gather | bytes 655360 | tf_op jit(solution)/shard_map/all_gather | solution.py:62
  42.8 0.1 convert_bitcast_fusion.1
  43.0 0.6 copy.156
  43.6 0.1 fusion.30
  43.7 2.4 maximum_reduce_fusion
  46.0 2.1 gather_fusion
  48.2 2.4 compare_reduce_fusion
  50.5 3.1 fusion.4
  53.7 13.7 %all-to-all-start.1 = ((bf16[128,1,64,128]{3,2,1,0:T(8,128)(2,1)}), bf16[128,1,64,128]{3,2,1,0:T(8,128)(2,1)S(1)}, u32[]{:S(2)}, u32[]{:S(2)}) async-start(bf16[128,1,64,128]{3,2,1,0:T(8,128)(2,1)} %fusion.4), calls=%async_computation.1 | async-start | bytes 4194304 | tf_op jit(solution)/shard_map/all_to_all | solution.py:77
  67.5 0.6 fusion.42
  68.1 0.7 fusion.32
  68.8 52.6 %all-to-all-done.1 = bf16[128,1,64,128]{3,2,1,0:T(8,128)(2,1)S(1)} async-done(((bf16[128,1,64,128]{3,2,1,0:T(8,128)(2,1)}), bf16[128,1,64,128]{3,2,1,0:T(8,128)(2,1)S(1)}, u32[]{:S(2)}, u32[]{:S(2)}) %all-to-all-start.1) | async-done | bytes 2097184 | tf_op jit(solution)/shard_map/all_to_all | solution.py:77
  121.4 1.2 gather_fusion.1
  122.6 1.0 fusion.28
  123.7 1.7 convolution_convert_fusion.3
  125.4 0.1 copy.97
  125.5 0.1 stack.37
  125.6 15.5 %all_to_all.34 = bf16[4,8,1,64,128]{4,1,3,2,0:T(8,128)(2,1)S(1)} all-to-all(bf16[4,8,1,64,128]{4,1,3,2,0:T(8,128)(2,1)S(1)} %stack.37), channel_id=1, replica_groups=mesh['area'=128,'blk'=4] {'blk'}, dimensions={0} | all-to-all | bytes 1048576 | tf_op jit(solution)/shard_map/all_to_all | solution.py:53
  141.1 31.5 %all-reduce.5.cloned.1.call-done = bf16[8,64,512]{2,0,1:T(8,128)(2,1)} async-done(((bf16[8,64,512]{2,0,1:T(8,128)(2,1)}), bf16[8,64,512]{2,0,1:T(8,128)(2,1)}) %all-reduce.5.cloned.1.call-update) | async-done | bytes 524304 | tf_op jit(solution)/shard_map/psum | solution.py:87
  172.7 1.7 tanh_convert_fusion.3
  174.4 2.1 gather_fusion.2
  176.6 1.8 fusion.3
  178.4 68.3 %all_to_all.35 = bf16[128,1,64,128]{3,2,1,0:T(8,128)(2,1)} all-to-all(bf16[128,1,64,128]{3,2,1,0:T(8,128)(2,1)S(1)} %fusion.3), channel_id=1, replica_groups=mesh['area'=128,'blk'=4] {'area'}, dimensions={0} | all-to-all | bytes 4194304 | tf_op jit(solution)/shard_map/all_to_all | solution.py:77
  246.7 2.2 gather_fusion.3
  248.9 0.2 fusion.26
  249.1 1.7 convolution_convert_fusion.2
  250.8 46.4 %all-reduce.7.cloned.1.call-done = bf16[8,64,512]{2,0,1:T(8,128)(2,1)} async-done(((bf16[8,64,512]{2,0,1:T(8,128)(2,1)}), bf16[8,64,512]{2,0,1:T(8,128)(2,1)}) %all-reduce.7.cloned.1.call-update) | async-done | bytes 524304 | tf_op jit(solution)/shard_map/psum | solution.py:87
  297.3 1.8 tanh_convert_fusion.2
  299.1 0.8 copy-done.4
  299.9 2.1 gather_fusion.4
  302.1 1.8 fusion.2
  303.9 68.1 %all_to_all.36 = bf16[128,1,64,128]{3,2,1,0:T(8,128)(2,1)} all-to-all(bf16[128,1,64,128]{3,2,1,0:T(8,128)(2,1)S(1)} %fusion.2), channel_id=1, replica_groups=mesh['area'=128,'blk'=4] {'area'}, dimensions={0} | all-to-all | bytes 4194304 | tf_op jit(solution)/shard_map/all_to_all | solution.py:77
  372.0 2.2 gather_fusion.5
  374.1 0.2 fusion.24
  374.3 1.7 convolution_convert_fusion.1
  376.0 46.4 %all-reduce.9.cloned.1.call-done = bf16[8,64,512]{2,0,1:T(8,128)(2,1)} async-done(((bf16[8,64,512]{2,0,1:T(8,128)(2,1)}), bf16[8,64,512]{2,0,1:T(8,128)(2,1)}) %all-reduce.9.cloned.1.call-update) | async-done | bytes 524304 | tf_op jit(solution)/shard_map/psum | solution.py:87
  422.4 2.0 tanh_convert_fusion.1
  424.4 0.8 copy-done.2
  425.3 2.1 gather_fusion.6
  427.4 3.1 fusion.1
  430.5 14.7 %all-to-all-start.5 = ((bf16[128,1,64,128]{3,2,1,0:T(8,128)(2,1)}), bf16[128,1,64,128]{3,2,1,0:T(8,128)(2,1)}, u32[]{:S(2)}, u32[]{:S(2)}) async-start(bf16[128,1,64,128]{3,2,1,0:T(8,128)(2,1)} %fusion.1), calls=%async_computation.5 | async-start | bytes 4194304 | tf_op jit(solution)/shard_map/all_to_all | solution.py:77
  445.3 0.3 all-reduce.11.cloned.1.call-start
  445.6 53.4 %all-to-all-done.5 = bf16[128,1,64,128]{3,2,1,0:T(8,128)(2,1)} async-done(((bf16[128,1,64,128]{3,2,1,0:T(8,128)(2,1)}), bf16[128,1,64,128]{3,2,1,0:T(8,128)(2,1)}, u32[]{:S(2)}, u32[]{:S(2)}) %all-to-all-start.5) | async-done | bytes 2097184 | tf_op jit(solution)/shard_map/all_to_all | solution.py:77
  499.0 2.2 gather_fusion.7
  501.1 0.2 fusion.22
  501.3 1.7 convolution_convert_fusion
  503.1 0.1 fusion.21
  503.2 0.7 copy.109
  503.8 45.5 %all-reduce.11.cloned.1.call-done = bf16[8,64,512]{2,0,1:T(8,128)(2,1)} async-done(((bf16[8,64,512]{2,0,1:T(8,128)(2,1)}), bf16[8,64,512]{2,0,1:T(8,128)(2,1)}) %all-reduce.11.cloned.1.call-update) | async-done | bytes 524304 | tf_op jit(solution)/shard_map/psum | solution.py:87
  549.4 2.5 fusion.16
  551.9 0.3 convert_reduce_fusion
  552.2 0.5 fusion
  552.7 0.7 copy.110
  553.5 0.8 copy.112
  554.2 0.6 gather_fusion.8
  554.8 1.1 fusion.7
  (46 shorter events, 0.5 us)
Async XLA Ops:
  7.2 115.5 %copy-start = (bf16[3,1,128,512]{3,2,1,0:T(8,128)(2,1)S(1)}, bf16[3,1,128,512]{3,2,1,0:T(8,128)(2,1)}, u32[]{:S(2)}) copy-start(bf16[3,1,128,512]{3,2,1,0:T(8,128)(2,1)} %param.9) | copy-start | bytes 1179652
  9.8 18.9 %copy-start.9 = (pred[3]{0:T(512)(128)(4,1)}, pred[3]{0:T(512)(128)(4,1)S(1)}, u32[]{:S(2)}) copy-start(pred[3]{0:T(512)(128)(4,1)S(1)} %get-tuple-element.19) | copy-start | bytes 13
  10.0 0.5 copy-start.11
  11.3 32.3 %all-to-all-start = ((s32[128,1,1]{2,1,0:T(1,128)}), s32[128,1,1]{2,1,0:T(1,128)S(1)}, u32[]{:S(2)}, u32[]{:S(2)}) async-start(s32[128,1,1]{2,1,0:T(1,128)} %copy.93), calls=%async_computation | async-start | bytes 131072 | tf_op jit(solution)/shard_map/all_to_all | solution.py:43
  53.7 67.8 %all-to-all-start.1 = ((bf16[128,1,64,128]{3,2,1,0:T(8,128)(2,1)}), bf16[128,1,64,128]{3,2,1,0:T(8,128)(2,1)S(1)}, u32[]{:S(2)}, u32[]{:S(2)}) async-start(bf16[128,1,64,128]{3,2,1,0:T(8,128)(2,1)} %fusion.4), calls=%async_computation.1 | async-start | bytes 4194304 | tf_op jit(solution)/shard_map/all_to_all | solution.py:77
  67.4 105.3 %all-reduce.5.cloned.1.call-start = ((), (), s32[]{:S(2)}) async-start(), calls=%async_computation.6 | async-start | bytes 1048576 | tf_op jit(solution)/shard_map/psum | solution.py:87
  122.6 2.8 copy-start.8
  125.4 171.9 %all-reduce.7.cloned.1.call-start = ((), (), s32[]{:S(2)}) async-start(), calls=%async_computation.7 | async-start | bytes 1048576 | tf_op jit(solution)/shard_map/psum | solution.py:87
  246.7 50.6 %copy-start.1 = (bf16[8,64,512]{2,0,1:T(8,128)(2,1)S(1)}, bf16[8,64,512]{2,0,1:T(8,128)(2,1)}, u32[]{:S(2)}) copy-start(bf16[8,64,512]{2,0,1:T(8,128)(2,1)} %all-reduce.5.cloned.1.call-done) | copy-start | bytes 1572868
  250.8 171.6 %all-reduce.9.cloned.1.call-start = ((), (), s32[]{:S(2)}) async-start(), calls=%async_computation.8 | async-start | bytes 1048576 | tf_op jit(solution)/shard_map/psum | solution.py:87
  299.1 0.8 copy-start.4
  424.4 0.8 copy-start.2
  430.5 15.0 %copy-start.12 = (s32[3]{0:T(128)S(1)}, s32[3]{0:T(128)}, u32[]{:S(2)}) copy-start(s32[3]{0:T(128)} %param.10) | copy-start | bytes 40
  430.5 68.4 %all-to-all-start.5 = ((bf16[128,1,64,128]{3,2,1,0:T(8,128)(2,1)}), bf16[128,1,64,128]{3,2,1,0:T(8,128)(2,1)}, u32[]{:S(2)}, u32[]{:S(2)}) async-start(bf16[128,1,64,128]{3,2,1,0:T(8,128)(2,1)} %fusion.1), calls=%async_computation.5 | async-start | bytes 4194304 | tf_op jit(solution)/shard_map/all_to_all | solution.py:77
  445.3 57.7 %copy-start.7 = (bf16[3,64,128]{2,1,0:T(8,128)(2,1)S(1)}, bf16[3,64,128]{2,1,0:T(8,128)(2,1)}, u32[]{:S(2)}) copy-start(bf16[3,64,128]{2,1,0:T(8,128)(2,1)} %gather_fusion.1) | copy-start | bytes 147460
  445.3 104.1 %all-reduce.11.cloned.1.call-start = ((), (), s32[]{:S(2)}) async-start(), calls=%async_computation.9 | async-start | bytes 1048576 | tf_op jit(solution)/shard_map/psum | solution.py:87
  549.4 2.5 copy-start.3
  549.4 2.5 copy-start.5
  553.4 1.4 copy-start.6
  553.4 1.4 copy-start.10
Sparse Core Ops, SparseCore 0:
  125.5 47.1 all-reduce.4
  250.9 46.3 all-reduce.6
  376.1 46.2 all-reduce.8
  503.1 46.2 all-reduce.10
